TPU v7x, 512 devices: a whole 4x8x8 slice. The times are simulated.
512 devices in a mesh: dp: 8 (over z), expert: 64 (over y, x, core).
Axes of the slice: x: 4, y: 8, z: 8, core: 2. Of those that a mesh axis runs over, the one named last changes fastest.
Arguments:
- tokens: bfloat16 [65536, 1024], P(('dp', 'expert')), may hold values from -6 to 6
- expert_ids: int32 [65536, 4], P(('dp', 'expert')), may hold values from 0 to 63, all different within a row; in each aligned block of 128 rows (0 to 127, 128 to 255, ...) at most 16 rows name the same one
- gate_probs: float32 [65536, 4], P(('dp', 'expert')), may hold values from 0.05 to 1
- gate_up: bfloat16 [64, 1024, 768], P('expert', 'dp'), may hold values from -0.1875 to 0.1875
- down_proj: bfloat16 [64, 384, 1024], P('expert', None, 'dp'), may hold values from -0.3125 to 0.3125
- cotangent: bfloat16 [65536, 1024], P(('dp', 'expert')), may hold values from -0.75 to 0.75
Outputs:
- moe_out: bfloat16 [65536, 1024], P(('dp', 'expert'))
- token_grads: bfloat16 [65536, 1024], P(('dp', 'expert'))
- gate_grads: float32 [65536, 4], P(('dp', 'expert'))
- gate_up_grads: float32 [64, 1024, 768], P('expert', 'dp')
- down_grads: float32 [64, 384, 1024], P('expert', None, 'dp')
Inputs may be any that keep to these rules, and one draw needn't show every extreme that they name: `expert_ids`: each row names 4 different experts. Among the rows of one device no expert is named more than 16 times, and in every draw some device names some expert exactly 16 times.
All inputs are finite; a program needn't handle non-finite values.
Results may differ from a plain program's by a relative error of at most 0.012.
Values may be sent and summed in bfloat16 or wider, within the bound.
No kernel may reach another device: no remote copies, remote signals or barrier semaphores. Data moves between devices by JAX's collectives and lax.ppermute only.
A program may use at most 64 MiB of HBM per device.

v0:
```python
import jax
import jax.numpy as jnp
from jax import lax
from jax.sharding import PartitionSpec as P


def forward_rows(rows_in, weight_in, weight_out):
    hidden_width = weight_out.shape[0]
    pre_act = jnp.dot(rows_in, weight_in, preferred_element_type=jnp.float32)
    hidden = (jax.nn.silu(pre_act[:, :hidden_width]) * pre_act[:, hidden_width:]).astype(
        jnp.bfloat16
    )
    expert_out = jnp.dot(hidden, weight_out, preferred_element_type=jnp.float32).astype(
        jnp.bfloat16
    )
    return (expert_out, pre_act, hidden)


def backward_rows(rows_in, grad_rows, pre_act, hidden, weight_in, weight_out):
    hidden_width = weight_out.shape[0]
    contract_last = (((1,), (1,)), ((), ()))
    contract_first = (((0,), (0,)), ((), ()))
    grad_hidden = lax.dot_general(
        grad_rows, weight_out, contract_last, preferred_element_type=jnp.float32
    )
    pre_gate = pre_act[:, :hidden_width]
    sigmoid_value = jax.nn.sigmoid(pre_gate)
    grad_gate = (
        grad_hidden
        * pre_act[:, hidden_width:]
        * sigmoid_value
        * (1.0 + pre_gate * (1.0 - sigmoid_value))
    )
    grad_up = grad_hidden * jax.nn.silu(pre_gate)
    grad_pre = jnp.concatenate([grad_gate, grad_up], axis=1).astype(jnp.bfloat16)
    grad_in = lax.dot_general(
        grad_pre, weight_in, contract_last, preferred_element_type=jnp.float32
    ).astype(jnp.bfloat16)
    weight_in_grad = lax.dot_general(
        rows_in, grad_pre, contract_first, preferred_element_type=jnp.float32
    )
    weight_out_grad = lax.dot_general(
        hidden, grad_rows, contract_first, preferred_element_type=jnp.float32
    )
    return (grad_in, weight_in_grad, weight_out_grad)


def live_slots(recv_counts, capacity):
    within = jnp.arange(capacity, dtype=jnp.int32)[None, :] < recv_counts[:, None]
    return within.reshape(-1)


def expert_forward(rows_in, filled, weight_in, weight_out):
    zero_row = jnp.zeros((), jnp.bfloat16)
    expert_out, pre_act, hidden = forward_rows(rows_in, weight_in, weight_out)
    expert_out = jnp.where(filled[:, None], expert_out, zero_row)
    stored = (rows_in, pre_act, hidden, None)
    return (expert_out, stored)


def expert_backward(grads_in, filled, stored, weight_in, weight_out):
    zero_row = jnp.zeros((), jnp.bfloat16)
    rows_in, pre_act, hidden, unused_plan = stored
    grad_back, in_grad, out_grad = backward_rows(
        rows_in, grads_in, pre_act, hidden, weight_in, weight_out
    )
    grad_back = jnp.where(filled[:, None], grad_back, zero_row)
    return (grad_back, in_grad, out_grad)


def local(tokens, expert_ids, gate_probs, gate_up, down_proj, cotangent):
    token_count, top_count = expert_ids.shape
    expert_count = lax.axis_size("expert")
    capacity = 2 * token_count * top_count // expert_count
    route_count = token_count * top_count
    slot_count = expert_count * capacity
    flat_ids = expert_ids.reshape(route_count)
    onehot = (flat_ids[:, None] == jnp.arange(expert_count, dtype=jnp.int32)[None, :]).astype(
        jnp.int32
    )
    slot_index = jnp.sum((jnp.cumsum(onehot, axis=0) - onehot) * onehot, axis=1)
    position = flat_ids * capacity + slot_index
    counts = jnp.sum(onehot, axis=0)
    slot_range = jnp.arange(slot_count, dtype=jnp.int32)
    matches = position[None, :] == slot_range[:, None]
    route_of_slot = jnp.sum(
        jnp.where(matches, jnp.arange(route_count, dtype=jnp.int32)[None, :], 0), axis=1
    )
    slot_filled = jnp.any(matches, axis=1)
    token_of_slot = route_of_slot // top_count
    zero_row = jnp.zeros((), jnp.bfloat16)
    send_tokens = jnp.where(slot_filled[:, None], tokens[token_of_slot], zero_row)
    slot_probs = jnp.where(slot_filled, gate_probs.reshape(route_count)[route_of_slot], 0.0)
    send_grads = (slot_probs[:, None] * cotangent[token_of_slot].astype(jnp.float32)).astype(
        jnp.bfloat16
    )
    weight_in, weight_out = (
        lax.all_gather(gate_up, "dp", axis=1, tiled=True),
        lax.all_gather(down_proj, "dp", axis=2, tiled=True),
    )
    weight_in = weight_in[0]
    weight_out = weight_out[0]
    rows_in, recv_counts = (
        lax.all_to_all(send_tokens, "expert", split_axis=0, concat_axis=0, tiled=True),
        lax.all_to_all(counts, "expert", split_axis=0, concat_axis=0, tiled=True),
    )
    filled = live_slots(recv_counts, capacity)
    expert_out, stored = expert_forward(rows_in, filled, weight_in, weight_out)
    back_out = lax.all_to_all(expert_out, "expert", split_axis=0, concat_axis=0, tiled=True)
    grads_in = lax.all_to_all(send_grads, "expert", split_axis=0, concat_axis=0, tiled=True)
    grad_back, in_grad, out_grad = expert_backward(grads_in, filled, stored, weight_in, weight_out)
    back_grad = lax.all_to_all(grad_back, "expert", split_axis=0, concat_axis=0, tiled=True)
    sum_in, sum_out = (
        lax.psum_scatter(
            in_grad[None].astype(jnp.bfloat16), "dp", scatter_dimension=1, tiled=True
        ).astype(jnp.float32),
        lax.psum_scatter(
            out_grad[None].astype(jnp.bfloat16), "dp", scatter_dimension=2, tiled=True
        ).astype(jnp.float32),
    )
    out_routes = back_out[position].reshape(token_count, top_count, -1).astype(jnp.float32)
    moe_out = jnp.sum(gate_probs[:, :, None] * out_routes, axis=1).astype(jnp.bfloat16)
    gate_grads = jnp.sum(cotangent.astype(jnp.float32)[:, None, :] * out_routes, axis=2)
    grad_routes = back_grad[position].reshape(token_count, top_count, -1).astype(jnp.float32)
    token_grads = jnp.sum(grad_routes, axis=1).astype(jnp.bfloat16)
    return (moe_out, token_grads, gate_grads, sum_in, sum_out)


def solution(mesh):
    return jax.shard_map(
        local,
        mesh=mesh,
        in_specs=(
            P(("dp", "expert"), None),
            P(("dp", "expert"), None),
            P(("dp", "expert"), None),
            P("expert", "dp", None),
            P("expert", None, "dp"),
            P(("dp", "expert"), None),
        ),
        out_specs=(
            P(("dp", "expert"), None),
            P(("dp", "expert"), None),
            P(("dp", "expert"), None),
            P("expert", "dp", None),
            P("expert", None, "dp"),
        ),
        check_vma=False,
    )
```

profile of v0, /device:TPU:2, one launch (start us, length us, event | category | flops | bytes accessed | tf_op | source)
XLA Modules:
  0.0 300.2 jit_solution(8653985739572995588)
XLA Ops:
  7.2 0.8 copy.35
  8.2 1.2 reduce-window.6
  9.5 0.2 slice_reduce_fusion
  9.7 0.2 fusion.12
  9.9 0.7 copy.36
  10.6 10.7 %all-to-all-start = ((s32[64,1,1]{2,1,0:T(1,128)}), s32[64,1,1]{2,1,0:T(1,128)S(1)}, u32[]{:S(2)}, u32[]{:S(2)}) async-start(s32[64,1,1]{2,1,0:T(1,128)} %copy.36), calls=%async_computation | async-start | bytes 65536 | tf_op jit(solution)/shard_map/all_to_all | solution.py:105
  21.3 0.3 select_reduce_fusion
  21.6 0.3 fusion.1
  22.0 4.1 %gather_fusion = bf16[1024,1024]{1,0:T(8,128)(2,1)S(1)} fusion(bf16[128,1024]{1,0:T(8,128)(2,1)S(1)} %copy-done, s32[1024]{0:T(1024)S(1)} %broadcast_clamp_fusion.1), kind=kCustom, calls=%fused_computation | custom fusion | bytes 4198400 | tf_op jit(solution)/shard_map/gather | solution.py:92
  26.1 1.6 broadcast_select_fusion
  27.7 2.2 all-to-all-done
  29.8 8.5 %all-to-all-start.1 = ((bf16[64,16,1024]{2,1,0:T(8,128)(2,1)}), bf16[64,16,1024]{2,1,0:T(8,128)(2,1)}, u32[]{:S(2)}, u32[]{:S(2)}) async-start(bf16[64,16,1024]{2,1,0:T(8,128)(2,1)} %broadcast_select_fusion), calls=%async_computation.1 | async-start | bytes 4194304 | tf_op jit(solution)/shard_map/all_to_all | solution.py:104
  38.3 0.1 copy.34
  38.5 6.9 %gather_fusion.2 = f32[1024]{0:T(1024)S(1)} fusion(f32[512]{0:T(512)S(1)} %reshape.204, s32[1024]{0:T(1024)S(1)} %broadcast_clamp_fusion), kind=kCustom, calls=%fused_computation.2 | custom fusion | bytes 12288 | tf_op jit(solution)/shard_map/gather | solution.py:93
  45.5 4.1 %gather_fusion.3 = bf16[1024,1024]{1,0:T(8,128)(2,1)S(1)} fusion(bf16[128,1024]{1,0:T(8,128)(2,1)S(1)} %copy-done.1, s32[1024]{0:T(1024)S(1)} %broadcast_clamp_fusion.1), kind=kCustom, calls=%fused_computation.3 | custom fusion | bytes 4198400 | tf_op jit(solution)/shard_map/gather | solution.py:94
  49.6 1.8 fusion
  51.4 38.1 %all-to-all-done.1 = bf16[64,16,1024]{2,1,0:T(8,128)(2,1)} async-done(((bf16[64,16,1024]{2,1,0:T(8,128)(2,1)}), bf16[64,16,1024]{2,1,0:T(8,128)(2,1)}, u32[]{:S(2)}, u32[]{:S(2)}) %all-to-all-start.1) | async-done | bytes 2097184 | tf_op jit(solution)/shard_map/all_to_all | solution.py:104
  89.4 5.4 %all-to-all-start.3 = ((bf16[64,16,1024]{2,1,0:T(8,128)(2,1)}), bf16[64,16,1024]{2,1,0:T(8,128)(2,1)S(1)}, u32[]{:S(2)}, u32[]{:S(2)}) async-start(bf16[64,16,1024]{2,1,0:T(8,128)(2,1)} %fusion), calls=%async_computation.3 | async-start | bytes 4194304 | tf_op jit(solution)/shard_map/all_to_all | solution.py:110
  94.9 0.7 all-gather.2.cloned.1.call-update
  95.6 34.6 %all_gather.7 = bf16[1,384,1024]{2,1,0:T(8,128)(2,1)S(1)} all-gather(bf16[1,384,128]{2,1,0:T(8,128)(2,1)} %param.10), channel_id=1, replica_groups=mesh['dp'=8,'expert'=64] {'dp'}, dimensions={2}, use_global_device_ids=true | all-gather | bytes 884736 | tf_op jit(solution)/shard_map/all_gather | solution.py:99
  130.2 1.2 reduce.5
  131.6 15.3 %all-gather.2.cloned.1.call-done = bf16[1,1024,768]{2,1,0:T(8,128)(2,1)} async-done(((bf16[1,128,768]{2,1,0:T(8,128)(2,1)}), bf16[1,1024,768]{2,1,0:T(8,128)(2,1)}) %all-gather.2.cloned.1.call-update) | async-done | bytes 1572880 | tf_op jit(solution)/shard_map/all_gather | solution.py:98
  146.9 5.5 %fusion.3 = f32[1024,768]{0,1:T(8,128)} fusion(bf16[1024,1024]{1,0:T(8,128)(2,1)} %bitcast.5, bf16[1,1024,768]{2,1,0:T(8,128)(2,1)} %all-gather.2.cloned.1.call-done), kind=kOutput, calls=%fused_computation.18 | convolution fusion | flops 1610612736 | bytes 6815744 | tf_op jit(solution)/shard_map/dot_general | solution.py:9
  152.5 5.1 %multiply_convert_fusion.1 = (bf16[1024,384]{0,1:T(8,128)(2,1)S(1)}, bf16[1024,384]{0,1:T(8,128)(2,1)S(1)}, bf16[1024,384]{0,1:T(8,128)(2,1)}) fusion(f32[1024,768]{0,1:T(8,128)} %fusion.3, bf16[1024,1024]{1,0:T(8,128)(2,1)S(1)} %bitcast.60, bf16[1,384,1024]{2,1,0:T(8,128)(2,1)S(1)} %all_gather.7), kind=kOutput, calls=%fused_computation.21 | convolution fusion | flops 811204608 | bytes 8388608 | tf_op jit(solution)/shard_map/dot_general | solution.py:23
  157.6 3.3 %convert_select_fusion = bf16[1024,1024]{1,0:T(8,128)(2,1)} fusion(pred[1024]{0:T(1024)(128)(4,1)S(1)} %lt.50, bf16[1,1024,768]{2,1,0:T(8,128)(2,1)S(1)} %copy-done.6, bf16[1024,384]{0,1:T(8,128)(2,1)S(1)} %get-tuple-element.25, bf16[1024,384]{0,1:T(8,128)(2,1)S(1)} %get-tuple-element.24), kind=kOutput, calls=%fused_computation.8 | convolution fusion | flops 1615855616 | bytes 5243904 | tf_op jit(solution)/shard_map/dot_general | solution.py:36
  160.9 10.3 %all-to-all-start.4 = ((bf16[64,16,1024]{2,1,0:T(8,128)(2,1)}), bf16[64,16,1024]{2,1,0:T(8,128)(2,1)S(1)}, u32[]{:S(2)}, u32[]{:S(2)}) async-start(bf16[64,16,1024]{2,1,0:T(8,128)(2,1)} %bitcast.62), calls=%async_computation.4 | async-start | bytes 4194304 | tf_op jit(solution)/shard_map/all_to_all | solution.py:112
  171.2 3.7 %fusion.7 = bf16[1,384,1024]{2,1,0:T(8,128)(2,1)} fusion(bf16[1024,384]{0,1:T(8,128)(2,1)} %get-tuple-element.26, bf16[1024,1024]{1,0:T(8,128)(2,1)} %bitcast.61), kind=kOutput, calls=%fused_computation.27 | convolution fusion | flops 805699584 | bytes 3670016 | tf_op jit(solution)/shard_map/dot_general | solution.py:42
  174.9 4.8 %copy.42 = bf16[1,384,1024]{1,0,2:T(2,128)(2,1)} copy(bf16[1,384,1024]{2,1,0:T(8,128)(2,1)} %fusion.7) | data formatting | bytes 1572864
  179.7 2.5 copy.48
  182.3 3.8 %convert_select_fusion.1 = bf16[1024,1024]{1,0:T(8,128)(2,1)} fusion(pred[1024]{0:T(1024)(128)(4,1)S(1)} %lt.50, bf16[1024,384]{0,1:T(8,128)(2,1)} %get-tuple-element.26, bf16[1,384,1024]{2,1,0:T(8,128)(2,1)S(1)} %all_gather.7), kind=kOutput, calls=%fused_computation.10 | convolution fusion | flops 807403520 | bytes 3671040 | tf_op jit(solution)/shard_map/dot_general | solution.py:13
  186.0 36.4 %all-to-all-done.4 = bf16[64,16,1024]{2,1,0:T(8,128)(2,1)S(1)} async-done(((bf16[64,16,1024]{2,1,0:T(8,128)(2,1)}), bf16[64,16,1024]{2,1,0:T(8,128)(2,1)S(1)}, u32[]{:S(2)}, u32[]{:S(2)}) %all-to-all-start.4) | async-done | bytes 2097184 | tf_op jit(solution)/shard_map/all_to_all | solution.py:112
  222.4 5.8 %all-to-all-start.2 = ((bf16[64,16,1024]{2,1,0:T(8,128)(2,1)}), bf16[64,16,1024]{2,1,0:T(8,128)(2,1)}, u32[]{:S(2)}, u32[]{:S(2)}) async-start(bf16[64,16,1024]{2,1,0:T(8,128)(2,1)} %bitcast.59), calls=%async_computation.2 | async-start | bytes 4194304 | tf_op jit(solution)/shard_map/all_to_all | solution.py:109
  228.2 0.3 reduce-scatter.5.cloned.1.call-start
  228.5 4.8 %fusion.6 = bf16[1,1024,768]{2,1,0:T(8,128)(2,1)} fusion(bf16[1024,1024]{1,0:T(8,128)(2,1)} %bitcast.5, bf16[1024,384]{0,1:T(8,128)(2,1)} %copy-done.9, bf16[1024,384]{0,1:T(8,128)(2,1)S(1)} %copy-done.8), kind=kOutput, calls=%fused_computation.25 | convolution fusion | flops 1614544896 | bytes 5242880 | tf_op jit(solution)/shard_map/dot_general | solution.py:39
  233.3 0.8 convert_element_type.75
  234.2 0.1 copy.39
  234.5 1.0 reshape_bitcast_fusion
  235.5 0.2 copy.43
  235.6 0.7 convert_element_type.81
  236.3 38.8 %reduce-scatter.5.cloned.1.call-done = bf16[1,128,768]{2,1,0:T(8,128)(2,1)} async-done(((bf16[1,1024,768]{2,1,0:T(8,128)(2,1)}), bf16[1,128,768]{2,1,0:T(8,128)(2,1)}) %reduce-scatter.5.cloned.1.call-update) | async-done | bytes 196624 | tf_op jit(solution)/shard_map/reduce_scatter | solution.py:114
  275.1 1.7 convert_element_type.78
  276.8 2.8 gather_fusion.4
  279.6 2.3 reshape.205
  281.9 4.6 %gather_fusion.1 = bf16[512,1024]{1,0:T(8,128)(2,1)S(1)} fusion(bf16[1024,1024]{1,0:T(8,128)(2,1)} %bitcast.9, s32[1024]{0:T(1024)S(1)} %pad_clamp_fusion), kind=kCustom, calls=%fused_computation.1 | custom fusion | bytes 2099200 | tf_op jit(solution)/shard_map/gather | solution.py:121
  286.5 0.7 reshape.206
  287.2 3.7 %multiply_reduce_fusion = (f32[128,4]{1,0:T(8,128)S(1)}, bf16[128,1024]{1,0:T(8,128)(2,1)}) fusion(f32[128,4,1024]{2,1,0:T(4,128)S(1)} %reshape.206, f32[128,1024]{1,0:T(8,128)} %convert_element_type.75, f32[128,4]{1,0:T(8,128)S(1)} %copy.34), kind=kLoop, calls=%fused_computation.7 | loop fusion | flops 1965568 | bytes 2887680 | tf_op jit(solution)/shard_map/reduce_sum | solution.py:123
  290.9 0.7 copy.41
  291.5 2.1 reduce_sum.67
  (46 shorter events, 1.1 us)
Async XLA Ops:
  7.2 14.8 %copy-start = (bf16[128,1024]{1,0:T(8,128)(2,1)S(1)}, bf16[128,1024]{1,0:T(8,128)(2,1)}, u32[]{:S(2)}) copy-start(bf16[128,1024]{1,0:T(8,128)(2,1)} %param.6) | copy-start | bytes 786436
  10.6 19.2 %all-to-all-start = ((s32[64,1,1]{2,1,0:T(1,128)}), s32[64,1,1]{2,1,0:T(1,128)S(1)}, u32[]{:S(2)}, u32[]{:S(2)}) async-start(s32[64,1,1]{2,1,0:T(1,128)} %copy.36), calls=%async_computation | async-start | bytes 65536 | tf_op jit(solution)/shard_map/all_to_all | solution.py:105
  27.7 10.6 %copy-start.5 = (f32[128,4]{0,1:T(4,128)S(1)}, f32[128,4]{0,1:T(4,128)}, u32[]{:S(2)}) copy-start(f32[128,4]{0,1:T(4,128)} %param.8) | copy-start | bytes 6148
  29.8 59.6 %all-to-all-start.1 = ((bf16[64,16,1024]{2,1,0:T(8,128)(2,1)}), bf16[64,16,1024]{2,1,0:T(8,128)(2,1)}, u32[]{:S(2)}, u32[]{:S(2)}) async-start(bf16[64,16,1024]{2,1,0:T(8,128)(2,1)} %broadcast_select_fusion), calls=%async_computation.1 | async-start | bytes 4194304 | tf_op jit(solution)/shard_map/all_to_all | solution.py:104
  38.5 7.0 %copy-start.1 = (bf16[128,1024]{1,0:T(8,128)(2,1)S(1)}, bf16[128,1024]{1,0:T(8,128)(2,1)}, u32[]{:S(2)}) copy-start(bf16[128,1024]{1,0:T(8,128)(2,1)} %param.11) | copy-start | bytes 786436
  89.4 63.0 %all-to-all-start.3 = ((bf16[64,16,1024]{2,1,0:T(8,128)(2,1)}), bf16[64,16,1024]{2,1,0:T(8,128)(2,1)S(1)}, u32[]{:S(2)}, u32[]{:S(2)}) async-start(bf16[64,16,1024]{2,1,0:T(8,128)(2,1)} %fusion), calls=%async_computation.3 | async-start | bytes 4194304 | tf_op jit(solution)/shard_map/all_to_all | solution.py:110
  94.9 52.0 %all-gather.2.cloned.1.call-start = ((), (), s32[]{:S(2)}) async-start(), calls=%async_computation.7 | async-start | bytes 1769472 | tf_op jit(solution)/shard_map/all_gather | solution.py:98
  152.5 5.1 %copy-start.3 = (bf16[64,16,1024]{2,1,0:T(8,128)(2,1)}, bf16[64,16,1024]{2,1,0:T(8,128)(2,1)S(1)}, u32[]{:S(2)}) copy-start(bf16[64,16,1024]{2,1,0:T(8,128)(2,1)S(1)} %all-to-all-done.3) | copy-start | bytes 6291460
  152.5 5.1 %copy-start.6 = (bf16[1,1024,768]{2,1,0:T(8,128)(2,1)S(1)}, bf16[1,1024,768]{2,1,0:T(8,128)(2,1)}, u32[]{:S(2)}) copy-start(bf16[1,1024,768]{2,1,0:T(8,128)(2,1)} %all-gather.2.cloned.1.call-done) | copy-start | bytes 4718596
  157.6 3.3 %copy-start.7 = (bf16[1024,384]{0,1:T(8,128)(2,1)}, bf16[1024,384]{0,1:T(8,128)(2,1)S(1)}, u32[]{:S(2)}) copy-start(bf16[1024,384]{0,1:T(8,128)(2,1)S(1)} %get-tuple-element.24) | copy-start | bytes 2359300
  157.6 3.3 %copy-start.9 = (bf16[1024,384]{0,1:T(8,128)(2,1)}, bf16[1024,384]{0,1:T(8,128)(2,1)S(1)}, u32[]{:S(2)}) copy-start(bf16[1024,384]{0,1:T(8,128)(2,1)S(1)} %get-tuple-element.25) | copy-start | bytes 2359300
  160.9 61.5 %all-to-all-start.4 = ((bf16[64,16,1024]{2,1,0:T(8,128)(2,1)}), bf16[64,16,1024]{2,1,0:T(8,128)(2,1)S(1)}, u32[]{:S(2)}, u32[]{:S(2)}) async-start(bf16[64,16,1024]{2,1,0:T(8,128)(2,1)} %bitcast.62), calls=%async_computation.4 | async-start | bytes 4194304 | tf_op jit(solution)/shard_map/all_to_all | solution.py:112
  171.2 63.3 %reduce-scatter.7.cloned.1.call-start = ((), (), s32[]{:S(2)}) async-start(), calls=%async_computation.9 | async-start | bytes 884736
  222.4 6.0 %copy-start.8 = (bf16[1024,384]{0,1:T(8,128)(2,1)S(1)}, bf16[1024,384]{0,1:T(8,128)(2,1)}, u32[]{:S(2)}) copy-start(bf16[1024,384]{0,1:T(8,128)(2,1)} %copy-done.7) | copy-start | bytes 2359300
  222.4 59.4 %all-to-all-start.2 = ((bf16[64,16,1024]{2,1,0:T(8,128)(2,1)}), bf16[64,16,1024]{2,1,0:T(8,128)(2,1)}, u32[]{:S(2)}, u32[]{:S(2)}) async-start(bf16[64,16,1024]{2,1,0:T(8,128)(2,1)} %bitcast.59), calls=%async_computation.2 | async-start | bytes 4194304 | tf_op jit(solution)/shard_map/all_to_all | solution.py:109
  228.2 46.9 %reduce-scatter.5.cloned.1.call-start = ((), (), s32[]{:S(2)}) async-start(), calls=%async_computation.8 | async-start | bytes 1769472 | tf_op jit(solution)/shard_map/reduce_scatter | solution.py:114
  233.3 0.9 copy-start.4
  287.2 4.4 %copy-start.2 = (bf16[128,4,1024]{2,1,0:T(4,128)(2,1)S(1)}, bf16[128,4,1024]{2,1,0:T(4,128)(2,1)}, u32[]{:S(2)}) copy-start(bf16[128,4,1024]{2,1,0:T(4,128)(2,1)} %reshape.205) | copy-start | bytes 3145732
Sparse Core Ops, SparseCore 0:
  97.8 49.0 all-gather.1
  182.4 39.1 reduce-scatter.6
  233.4 41.6 reduce-scatter.4
where the time goes:
time: 301 us; the launch traced here: 300 us
  waiting for transfers between devices  131 us (44%)
  starting transfers between devices  40.9 us (14%)
  local copies, waits for them, and re-layouts  37.2 us (12%)
  blocking collectives  34.6 us (11%)
  matrix products  26.3 us (9%)
  other arithmetic  15.8 us (5%)
  between operations  14 us (5%)
    reduce_scatter x1, waiting for transfers between devices, local(): lax.psum_scatter(in_grad[None].astype(jnp.bfloat16), 'dp', scatter_dimens...  38.8 us
    all_to_all x1, waiting for transfers between devices, local(): lax.all_to_all(send_tokens, 'expert', split_axis=0, concat_axis=0, tiled=...  38.1 us
    all_to_all x1, waiting for transfers between devices, local(): lax.all_to_all(grad_back, 'expert', split_axis=0, concat_axis=0, tiled=True)  36.4 us
    all_gather x1, blocking collectives, local(): lax.all_gather(down_proj, 'dp', axis=2, tiled=True)  34.6 us
    all_gather x1, waiting for transfers between devices, local(): lax.all_gather(gate_up, 'dp', axis=1, tiled=True)  15.3 us
    all_to_all x1, starting transfers between devices, local(): lax.all_to_all(counts, 'expert', split_axis=0, concat_axis=0, tiled=True)  10.7 us
    all_to_all x1, starting transfers between devices, local(): lax.all_to_all(grad_back, 'expert', split_axis=0, concat_axis=0, tiled=True)  10.3 us
    unnamed x27, local copies, waits for them, and re-layouts  10.1 us
  transfers between devices with their start and end apart: 8, of which 5 were waited for; matrix products, arithmetic and copies ran while one was open for 19% of the time, Pallas kernels for 0%

commit v1 on v0

--- a/solution.py
+++ b/solution.py
@@ -2,6 +2,27 @@
 import jax.numpy as jnp
 from jax import lax
 from jax.sharding import PartitionSpec as P
+
+
+def ring_gather(x, axis, dim):
+    size, index, span = (lax.axis_size(axis), lax.axis_index(axis), x.shape[dim])
+    right = [(i, (i + 1) % size) for i in range(size)]
+    behind = [(i, (i - 1) % size) for i in range(size)]
+    out = jnp.zeros((*x.shape[:dim], size * span, *x.shape[dim + 1 :]), x.dtype)
+    out = lax.dynamic_update_slice_in_dim(out, x, index * span, axis=dim)
+    from_left = from_right = x
+    middle = size // 2
+    for step in range(1, middle + 1):
+        from_left = lax.ppermute(from_left, axis, right)
+        out = lax.dynamic_update_slice_in_dim(
+            out, from_left, (index - step) % size * span, axis=dim
+        )
+        if step < size - middle:
+            from_right = lax.ppermute(from_right, axis, behind)
+            out = lax.dynamic_update_slice_in_dim(
+                out, from_right, (index + step) % size * span, axis=dim
+            )
+    return out
 
 
 def forward_rows(rows_in, weight_in, weight_out):
@@ -95,7 +116,7 @@
         jnp.bfloat16
     )
     weight_in, weight_out = (
-        lax.all_gather(gate_up, "dp", axis=1, tiled=True),
+        ring_gather(gate_up, "dp", 1),
         lax.all_gather(down_proj, "dp", axis=2, tiled=True),
     )
     weight_in = weight_in[0]

time: 301 us -> 323 us (1.073)
  starting transfers between devices: 40.9 us -> 69.7 us
  local copies, waits for them, and re-layouts: 37.2 us -> 48.3 us
  blocking collectives: 34.6 us -> 25.3 us
  waiting for transfers between devices: 131 us -> 122 us
    ppermute x0 -> x7, starting transfers between devices: none -> 29.1 us  [the longest x3 18.5 us: ring_gather(): from_right = lax.ppermute(from_right, axis, behind)]
    all_gather x1 -> x0, waiting for transfers between devices: 15.3 us -> none  [local(): lax.all_gather(gate_up, 'dp', axis=1, tiled=True)]
    all_gather x1, blocking collectives: 34.6 us -> 25.3 us  [local(): lax.all_gather(down_proj, 'dp', axis=2, tiled=True)]
    dynamic_update_slice x0 -> x8, local copies, waits for them, and re-layouts: none -> 8.31 us  [the longest x4 3.7 us: ring_gather(): lax.dynamic_update_slice_in_dim(out, from_left, (index - step) % size * s...]
    ppermute x0 -> x7, waiting for transfers between devices: none -> 5.65 us  [the longest x4 5.64 us: ring_gather(): from_left = lax.ppermute(from_left, axis, right)]
    unnamed x27 -> x23, local copies, waits for them, and re-layouts: 10.1 us -> 10.7 us
  transfers between devices with their start and end apart: 8 -> 14, of which waited for: 5 -> 6; matrix products, arithmetic and copies ran while one was open for 19% -> 20% of each run, Pallas kernels for 0% -> 0%
where the time goes in v1:
time: 323 us; the launch traced here: 322 us
  waiting for transfers between devices  122 us (38%)
  starting transfers between devices  69.7 us (22%)
  local copies, waits for them, and re-layouts  48.3 us (15%)
  matrix products  28.3 us (9%)
  blocking collectives  25.3 us (8%)
  between operations  14.5 us (4%)
  other arithmetic  13.8 us (4%)
    reduce_scatter x1, waiting for transfers between devices, local(): lax.psum_scatter(in_grad[None].astype(jnp.bfloat16), 'dp', scatter_dimens...  39.7 us
    all_to_all x1, waiting for transfers between devices, local(): lax.all_to_all(send_tokens, 'expert', split_axis=0, concat_axis=0, tiled=...  38.1 us
    all_to_all x1, waiting for transfers between devices, local(): lax.all_to_all(grad_back, 'expert', split_axis=0, concat_axis=0, tiled=True)  36.4 us
    all_gather x1, blocking collectives, local(): lax.all_gather(down_proj, 'dp', axis=2, tiled=True)  25.3 us
    ppermute x3, starting transfers between devices, ring_gather(): from_right = lax.ppermute(from_right, axis, behind)  18.5 us
    unnamed x23, local copies, waits for them, and re-layouts  10.7 us
    all_to_all x1, starting transfers between devices, local(): lax.all_to_all(counts, 'expert', split_axis=0, concat_axis=0, tiled=True)  10.7 us
    ppermute x4, starting transfers between devices, ring_gather(): from_left = lax.ppermute(from_left, axis, right)  10.5 us
  transfers between devices with their start and end apart: 14, of which 6 were waited for; matrix products, arithmetic and copies ran while one was open for 20% of the time, Pallas kernels for 0%

profile of v1, /device:TPU:2, one launch (start us, length us, event | category | flops | bytes accessed | tf_op | source)
XLA Modules:
  0.0 321.9 jit_solution(8610029935241159874)
XLA Ops:
  7.2 0.8 copy.35
  8.2 1.2 reduce-window.6
  9.9 0.7 copy.36
  10.6 10.7 %all-to-all-start = ((s32[64,1,1]{2,1,0:T(1,128)}), s32[64,1,1]{2,1,0:T(1,128)S(1)}, u32[]{:S(2)}, u32[]{:S(2)}) async-start(s32[64,1,1]{2,1,0:T(1,128)} %copy.36), calls=%async_computation | async-start | bytes 65536 | tf_op jit(solution)/shard_map/all_to_all | solution.py:126
  22.0 4.1 %gather_fusion = bf16[1024,1024]{1,0:T(8,128)(2,1)S(1)} fusion(bf16[128,1024]{1,0:T(8,128)(2,1)S(1)} %copy-done, s32[1024]{0:T(1024)S(1)} %broadcast_clamp_fusion.1), kind=kCustom, calls=%fused_computation | custom fusion | bytes 4198400 | tf_op jit(solution)/shard_map/gather | solution.py:113
  26.1 1.5 broadcast_select_fusion
  27.6 2.2 all-to-all-done
  29.8 8.4 %all-to-all-start.1 = ((bf16[64,16,1024]{2,1,0:T(8,128)(2,1)}), bf16[64,16,1024]{2,1,0:T(8,128)(2,1)}, u32[]{:S(2)}, u32[]{:S(2)}) async-start(bf16[64,16,1024]{2,1,0:T(8,128)(2,1)} %broadcast_select_fusion), calls=%async_computation.1 | async-start | bytes 4194304 | tf_op jit(solution)/shard_map/all_to_all | solution.py:125
  38.5 6.9 %gather_fusion.2 = f32[1024]{0:T(1024)S(1)} fusion(f32[512]{0:T(512)S(1)} %reshape.220, s32[1024]{0:T(1024)S(1)} %broadcast_clamp_fusion), kind=kCustom, calls=%fused_computation.2 | custom fusion | bytes 12288 | tf_op jit(solution)/shard_map/gather | solution.py:114
  45.5 4.1 %gather_fusion.3 = bf16[1024,1024]{1,0:T(8,128)(2,1)S(1)} fusion(bf16[128,1024]{1,0:T(8,128)(2,1)S(1)} %copy-done.1, s32[1024]{0:T(1024)S(1)} %broadcast_clamp_fusion.1), kind=kCustom, calls=%fused_computation.3 | custom fusion | bytes 4198400 | tf_op jit(solution)/shard_map/gather | solution.py:115
  49.6 1.8 fusion
  51.3 38.1 %all-to-all-done.1 = bf16[64,16,1024]{2,1,0:T(8,128)(2,1)} async-done(((bf16[64,16,1024]{2,1,0:T(8,128)(2,1)}), bf16[64,16,1024]{2,1,0:T(8,128)(2,1)}, u32[]{:S(2)}, u32[]{:S(2)}) %all-to-all-start.1) | async-done | bytes 2097184 | tf_op jit(solution)/shard_map/all_to_all | solution.py:125
  89.4 5.4 %all-to-all-start.3 = ((bf16[64,16,1024]{2,1,0:T(8,128)(2,1)}), bf16[64,16,1024]{2,1,0:T(8,128)(2,1)S(1)}, u32[]{:S(2)}, u32[]{:S(2)}) async-start(bf16[64,16,1024]{2,1,0:T(8,128)(2,1)} %fusion), calls=%async_computation.3 | async-start | bytes 4194304 | tf_op jit(solution)/shard_map/all_to_all | solution.py:131
  94.9 4.3 %collective-permute-start = (bf16[1,128,768]{2,1,0:T(8,128)(2,1)}, bf16[1,128,768]{2,1,0:T(8,128)(2,1)}, u32[]{:S(2)}, u32[]{:S(2)}) collective-permute-start(bf16[1,128,768]{2,1,0:T(8,128)(2,1)} %param.9), channel_id=1, source_target_pairs={{0,64},{64,128},{128,192},{192,256},{256,320},{320,384},{384,448},... | collective-permute-start | bytes 589832 | tf_op jit(solution)/shard_map/ppermute | solution.py:16
  99.1 8.6 %collective-permute-start.1 = (bf16[1,128,768]{2,1,0:T(8,128)(2,1)}, bf16[1,128,768]{2,1,0:T(8,128)(2,1)}, u32[]{:S(2)}, u32[]{:S(2)}) collective-permute-start(bf16[1,128,768]{2,1,0:T(8,128)(2,1)} %param.9), channel_id=1, source_target_pairs={{0,448},{64,0},{128,64},{192,128},{256,192},{320,256},{384,320},{4... | collective-permute-start | bytes 589832 | tf_op jit(solution)/shard_map/ppermute | solution.py:21
  107.9 1.3 squeeze.22
  109.1 1.6 bitcast_dynamic-update-slice_fusion.7
  110.8 25.3 %all_gather.3 = bf16[1,384,1024]{2,1,0:T(8,128)(2,1)S(1)} all-gather(bf16[1,384,128]{2,1,0:T(8,128)(2,1)} %param.10), channel_id=1, replica_groups=mesh['dp'=8,'expert'=64] {'dp'}, dimensions={2}, use_global_device_ids=true | all-gather | bytes 884736 | tf_op jit(solution)/shard_map/all_gather | solution.py:120
  136.1 1.2 reduce.5
  137.5 2.2 collective-permute-start.2
  139.7 4.8 %collective-permute-start.3 = (bf16[1,128,768]{2,1,0:T(8,128)(2,1)}, bf16[1,128,768]{2,1,0:T(8,128)(2,1)S(1)}, u32[]{:S(2)}, u32[]{:S(2)}) collective-permute-start(bf16[1,128,768]{2,1,0:T(8,128)(2,1)} %collective-permute-done.1), channel_id=1, source_target_pairs={{0,448},{64,0},{128,64},{192,128},{256,192},{320,256},{384,320},{4... | collective-permute-start | bytes 589832 | tf_op jit(solution)/shard_map/ppermute | solution.py:21
  144.6 1.6 bitcast_dynamic-update-slice_fusion.6
  146.2 1.6 bitcast_dynamic-update-slice_fusion.5
  147.8 1.9 collective-permute-start.4
  149.7 5.1 %collective-permute-start.5 = (bf16[1,128,768]{2,1,0:T(8,128)(2,1)S(1)}, bf16[1,128,768]{2,1,0:T(8,128)(2,1)S(1)}, u32[]{:S(2)}, u32[]{:S(2)}) collective-permute-start(bf16[1,128,768]{2,1,0:T(8,128)(2,1)S(1)} %collective-permute-done.3), channel_id=1, source_target_pairs={{0,448},{64,0},{128,64},{192,128},{256,192},{320,256},{384,320},{4... | collective-permute-start | bytes 589832 | tf_op jit(solution)/shard_map/ppermute | solution.py:21
  156.6 2.1 collective-permute-start.6
  158.7 0.7 bitcast_dynamic-update-slice_fusion.2
  160.1 5.3 %collective-permute-done.6 = bf16[1,128,768]{2,1,0:T(8,128)(2,1)S(1)} collective-permute-done((bf16[1,128,768]{2,1,0:T(8,128)(2,1)S(1)}, bf16[1,128,768]{2,1,0:T(8,128)(2,1)S(1)}, u32[]{:S(2)}, u32[]{:S(2)}) %collective-permute-start.6) | collective-permute-done | bytes 196640 | tf_op jit(solution)/shard_map/ppermute | solution.py:16
  166.1 5.6 %fusion.13 = f32[1024,768]{0,1:T(8,128)} fusion(bf16[1024,1024]{1,0:T(8,128)(2,1)} %bitcast.5, bf16[1024,768]{1,0:T(8,128)(2,1)} %bitcast_dynamic-update-slice_fusion), kind=kOutput, calls=%fused_computation.64 | convolution fusion | flops 1610612736 | bytes 6815744 | tf_op jit(solution)/shard_map/dot_general | solution.py:30
  171.7 5.0 %multiply_convert_fusion.1 = (bf16[1024,384]{0,1:T(8,128)(2,1)S(1)}, bf16[1024,384]{0,1:T(8,128)(2,1)S(1)}, bf16[1024,384]{0,1:T(8,128)(2,1)}) fusion(f32[1024,768]{0,1:T(8,128)} %fusion.13, bf16[1024,1024]{1,0:T(8,128)(2,1)S(1)} %bitcast.72, bf16[1,384,1024]{2,1,0:T(8,128)(2,1)S(1)} %all_gather.3), kind=kOutput, calls=%fused_computation.18 | convolution fusion | flops 811204608 | bytes 8388608 | tf_op jit(solution)/shard_map/dot_general | solution.py:44
  176.7 5.3 %convert_select_fusion = bf16[1024,1024]{1,0:T(8,128)(2,1)} fusion(pred[1024]{0:T(1024)(128)(4,1)S(1)} %lt.104, bf16[1024,768]{1,0:T(8,128)(2,1)} %bitcast_dynamic-update-slice_fusion, bf16[1024,384]{0,1:T(8,128)(2,1)S(1)} %get-tuple-element.25, bf16[1024,384]{0,1:T(8,128)(2,1)S(1)} %get-tuple-element.24), kind=kOutput, calls=%fused_computation.8 | convolution fusion | flops 1615855616 | bytes 5243904 | tf_op jit(solution)/shard_map/dot_general | solution.py:57
  182.1 10.1 %all-to-all-start.4 = ((bf16[64,16,1024]{2,1,0:T(8,128)(2,1)}), bf16[64,16,1024]{2,1,0:T(8,128)(2,1)S(1)}, u32[]{:S(2)}, u32[]{:S(2)}) async-start(bf16[64,16,1024]{2,1,0:T(8,128)(2,1)} %bitcast.75), calls=%async_computation.4 | async-start | bytes 4194304 | tf_op jit(solution)/shard_map/all_to_all | solution.py:133
  192.2 3.7 %fusion.4 = bf16[1,384,1024]{2,1,0:T(8,128)(2,1)} fusion(bf16[1024,384]{0,1:T(8,128)(2,1)} %get-tuple-element.26, bf16[1024,1024]{1,0:T(8,128)(2,1)} %bitcast.73), kind=kOutput, calls=%fused_computation.24 | convolution fusion | flops 805699584 | bytes 3670016 | tf_op jit(solution)/shard_map/dot_general | solution.py:63
  195.9 4.8 %copy.42 = bf16[1,384,1024]{1,0,2:T(2,128)(2,1)} copy(bf16[1,384,1024]{2,1,0:T(8,128)(2,1)} %fusion.4) | data formatting | bytes 1572864
  200.8 2.4 copy.48
  203.2 3.8 %convert_select_fusion.1 = bf16[1024,1024]{1,0:T(8,128)(2,1)} fusion(pred[1024]{0:T(1024)(128)(4,1)S(1)} %lt.104, bf16[1024,384]{0,1:T(8,128)(2,1)} %get-tuple-element.26, bf16[1,384,1024]{2,1,0:T(8,128)(2,1)S(1)} %all_gather.3), kind=kOutput, calls=%fused_computation.10 | convolution fusion | flops 807403520 | bytes 3671040 | tf_op jit(solution)/shard_map/dot_general | solution.py:34
  207.0 36.4 %all-to-all-done.4 = bf16[64,16,1024]{2,1,0:T(8,128)(2,1)S(1)} async-done(((bf16[64,16,1024]{2,1,0:T(8,128)(2,1)}), bf16[64,16,1024]{2,1,0:T(8,128)(2,1)S(1)}, u32[]{:S(2)}, u32[]{:S(2)}) %all-to-all-start.4) | async-done | bytes 2097184 | tf_op jit(solution)/shard_map/all_to_all | solution.py:133
  243.4 5.8 %all-to-all-start.2 = ((bf16[64,16,1024]{2,1,0:T(8,128)(2,1)}), bf16[64,16,1024]{2,1,0:T(8,128)(2,1)}, u32[]{:S(2)}, u32[]{:S(2)}) async-start(bf16[64,16,1024]{2,1,0:T(8,128)(2,1)} %bitcast.74), calls=%async_computation.2 | async-start | bytes 4194304 | tf_op jit(solution)/shard_map/all_to_all | solution.py:130
  249.4 4.8 %fusion.3 = bf16[1,1024,768]{2,1,0:T(8,128)(2,1)} fusion(bf16[1024,1024]{1,0:T(8,128)(2,1)} %bitcast.5, bf16[1024,384]{0,1:T(8,128)(2,1)} %copy-done.7, bf16[1024,384]{0,1:T(8,128)(2,1)S(1)} %copy-done.6), kind=kOutput, calls=%fused_computation.22 | convolution fusion | flops 1614544896 | bytes 5242880 | tf_op jit(solution)/shard_map/dot_general | solution.py:60
  255.2 1.0 reshape_bitcast_fusion
  257.1 39.7 %reduce-scatter.5.cloned.1.call-done = bf16[1,128,768]{2,1,0:T(8,128)(2,1)} async-done(((bf16[1,1024,768]{2,1,0:T(8,128)(2,1)}), bf16[1,128,768]{2,1,0:T(8,128)(2,1)}) %reduce-scatter.5.cloned.1.call-update) | async-done | bytes 196624 | tf_op jit(solution)/shard_map/reduce_scatter | solution.py:135
  296.7 1.7 convert_element_type.78
  298.4 2.8 gather_fusion.4
  301.2 1.5 reshape.221
  302.7 2.1 reduce_sum.67
  304.8 5.3 %gather_fusion.1 = bf16[512,1024]{1,0:T(8,128)(2,1)} fusion(bf16[1024,1024]{1,0:T(8,128)(2,1)} %bitcast.16, s32[1024]{0:T(1024)S(1)} %pad_clamp_fusion), kind=kCustom, calls=%fused_computation.1 | custom fusion | bytes 2099200 | tf_op jit(solution)/shard_map/gather | solution.py:142
  310.1 1.7 reshape.222
  311.9 2.6 multiply_reduce_fusion
  (62 shorter events, 7.8 us)
Async XLA Ops:
  7.2 14.8 %copy-start = (bf16[128,1024]{1,0:T(8,128)(2,1)S(1)}, bf16[128,1024]{1,0:T(8,128)(2,1)}, u32[]{:S(2)}) copy-start(bf16[128,1024]{1,0:T(8,128)(2,1)} %param.6) | copy-start | bytes 786436
  10.6 19.2 %all-to-all-start = ((s32[64,1,1]{2,1,0:T(1,128)}), s32[64,1,1]{2,1,0:T(1,128)S(1)}, u32[]{:S(2)}, u32[]{:S(2)}) async-start(s32[64,1,1]{2,1,0:T(1,128)} %copy.36), calls=%async_computation | async-start | bytes 65536 | tf_op jit(solution)/shard_map/all_to_all | solution.py:126
  27.6 10.6 %copy-start.4 = (f32[128,4]{0,1:T(4,128)S(1)}, f32[128,4]{0,1:T(4,128)}, u32[]{:S(2)}) copy-start(f32[128,4]{0,1:T(4,128)} %param.8) | copy-start | bytes 6148
  29.8 59.6 %all-to-all-start.1 = ((bf16[64,16,1024]{2,1,0:T(8,128)(2,1)}), bf16[64,16,1024]{2,1,0:T(8,128)(2,1)}, u32[]{:S(2)}, u32[]{:S(2)}) async-start(bf16[64,16,1024]{2,1,0:T(8,128)(2,1)} %broadcast_select_fusion), calls=%async_computation.1 | async-start | bytes 4194304 | tf_op jit(solution)/shard_map/all_to_all | solution.py:125
  38.5 7.0 %copy-start.1 = (bf16[128,1024]{1,0:T(8,128)(2,1)S(1)}, bf16[128,1024]{1,0:T(8,128)(2,1)}, u32[]{:S(2)}) copy-start(bf16[128,1024]{1,0:T(8,128)(2,1)} %param.11) | copy-start | bytes 786436
  89.4 82.3 %all-to-all-start.3 = ((bf16[64,16,1024]{2,1,0:T(8,128)(2,1)}), bf16[64,16,1024]{2,1,0:T(8,128)(2,1)S(1)}, u32[]{:S(2)}, u32[]{:S(2)}) async-start(bf16[64,16,1024]{2,1,0:T(8,128)(2,1)} %fusion), calls=%async_computation.3 | async-start | bytes 4194304 | tf_op jit(solution)/shard_map/all_to_all | solution.py:131
  94.9 42.6 %collective-permute-start = (bf16[1,128,768]{2,1,0:T(8,128)(2,1)}, bf16[1,128,768]{2,1,0:T(8,128)(2,1)}, u32[]{:S(2)}, u32[]{:S(2)}) collective-permute-start(bf16[1,128,768]{2,1,0:T(8,128)(2,1)} %param.9), channel_id=1, source_target_pairs={{0,64},{64,128},{128,192},{192,256},{256,320},{320,384},{384,448},... | collective-permute-start | bytes 589832 | tf_op jit(solution)/shard_map/ppermute | solution.py:16
  99.1 40.6 %collective-permute-start.1 = (bf16[1,128,768]{2,1,0:T(8,128)(2,1)}, bf16[1,128,768]{2,1,0:T(8,128)(2,1)}, u32[]{:S(2)}, u32[]{:S(2)}) collective-permute-start(bf16[1,128,768]{2,1,0:T(8,128)(2,1)} %param.9), channel_id=1, source_target_pairs={{0,448},{64,0},{128,64},{192,128},{256,192},{320,256},{384,320},{4... | collective-permute-start | bytes 589832 | tf_op jit(solution)/shard_map/ppermute | solution.py:21
  137.5 10.3 %collective-permute-start.2 = (bf16[1,128,768]{2,1,0:T(8,128)(2,1)}, bf16[1,128,768]{2,1,0:T(8,128)(2,1)S(1)}, u32[]{:S(2)}, u32[]{:S(2)}) collective-permute-start(bf16[1,128,768]{2,1,0:T(8,128)(2,1)} %collective-permute-done), channel_id=1, source_target_pairs={{0,64},{64,128},{128,192},{192,256},{256,320},{320,384},{384,448},... | collective-permute-start | bytes 589832 | tf_op jit(solution)/shard_map/ppermute | solution.py:16
  139.7 10.0 %collective-permute-start.3 = (bf16[1,128,768]{2,1,0:T(8,128)(2,1)}, bf16[1,128,768]{2,1,0:T(8,128)(2,1)S(1)}, u32[]{:S(2)}, u32[]{:S(2)}) collective-permute-start(bf16[1,128,768]{2,1,0:T(8,128)(2,1)} %collective-permute-done.1), channel_id=1, source_target_pairs={{0,448},{64,0},{128,64},{192,128},{256,192},{320,256},{384,320},{4... | collective-permute-start | bytes 589832 | tf_op jit(solution)/shard_map/ppermute | solution.py:21
  147.8 8.8 %collective-permute-start.4 = (bf16[1,128,768]{2,1,0:T(8,128)(2,1)S(1)}, bf16[1,128,768]{2,1,0:T(8,128)(2,1)S(1)}, u32[]{:S(2)}, u32[]{:S(2)}) collective-permute-start(bf16[1,128,768]{2,1,0:T(8,128)(2,1)S(1)} %collective-permute-done.2), channel_id=1, source_target_pairs={{0,64},{64,128},{128,192},{192,256},{256,320},{320,384},{384,448},... | collective-permute-start | bytes 589832 | tf_op jit(solution)/shard_map/ppermute | solution.py:16
  149.7 9.7 %collective-permute-start.5 = (bf16[1,128,768]{2,1,0:T(8,128)(2,1)S(1)}, bf16[1,128,768]{2,1,0:T(8,128)(2,1)S(1)}, u32[]{:S(2)}, u32[]{:S(2)}) collective-permute-start(bf16[1,128,768]{2,1,0:T(8,128)(2,1)S(1)} %collective-permute-done.3), channel_id=1, source_target_pairs={{0,448},{64,0},{128,64},{192,128},{256,192},{320,256},{384,320},{4... | collective-permute-start | bytes 589832 | tf_op jit(solution)/shard_map/ppermute | solution.py:21
  156.6 8.8 %collective-permute-start.6 = (bf16[1,128,768]{2,1,0:T(8,128)(2,1)S(1)}, bf16[1,128,768]{2,1,0:T(8,128)(2,1)S(1)}, u32[]{:S(2)}, u32[]{:S(2)}) collective-permute-start(bf16[1,128,768]{2,1,0:T(8,128)(2,1)S(1)} %collective-permute-done.4), channel_id=1, source_target_pairs={{0,64},{64,128},{128,192},{192,256},{256,320},{320,384},{384,448},... | collective-permute-start | bytes 589832 | tf_op jit(solution)/shard_map/ppermute | solution.py:16
  171.7 5.0 %copy-start.2 = (bf16[64,16,1024]{2,1,0:T(8,128)(2,1)}, bf16[64,16,1024]{2,1,0:T(8,128)(2,1)S(1)}, u32[]{:S(2)}) copy-start(bf16[64,16,1024]{2,1,0:T(8,128)(2,1)S(1)} %all-to-all-done.3) | copy-start | bytes 6291460
  176.7 5.3 %copy-start.5 = (bf16[1024,384]{0,1:T(8,128)(2,1)}, bf16[1024,384]{0,1:T(8,128)(2,1)S(1)}, u32[]{:S(2)}) copy-start(bf16[1024,384]{0,1:T(8,128)(2,1)S(1)} %get-tuple-element.24) | copy-start | bytes 2359300
  176.7 5.3 %copy-start.7 = (bf16[1024,384]{0,1:T(8,128)(2,1)}, bf16[1024,384]{0,1:T(8,128)(2,1)S(1)}, u32[]{:S(2)}) copy-start(bf16[1024,384]{0,1:T(8,128)(2,1)S(1)} %get-tuple-element.25) | copy-start | bytes 2359300
  182.1 61.3 %all-to-all-start.4 = ((bf16[64,16,1024]{2,1,0:T(8,128)(2,1)}), bf16[64,16,1024]{2,1,0:T(8,128)(2,1)S(1)}, u32[]{:S(2)}, u32[]{:S(2)}) async-start(bf16[64,16,1024]{2,1,0:T(8,128)(2,1)} %bitcast.75), calls=%async_computation.4 | async-start | bytes 4194304 | tf_op jit(solution)/shard_map/all_to_all | solution.py:133
  192.2 63.0 %reduce-scatter.7.cloned.1.call-start = ((), (), s32[]{:S(2)}) async-start(), calls=%async_computation.8 | async-start | bytes 884736
  243.4 6.0 %copy-start.6 = (bf16[1024,384]{0,1:T(8,128)(2,1)S(1)}, bf16[1024,384]{0,1:T(8,128)(2,1)}, u32[]{:S(2)}) copy-start(bf16[1024,384]{0,1:T(8,128)(2,1)} %copy-done.5) | copy-start | bytes 2359300
  243.4 61.4 %all-to-all-start.2 = ((bf16[64,16,1024]{2,1,0:T(8,128)(2,1)}), bf16[64,16,1024]{2,1,0:T(8,128)(2,1)}, u32[]{:S(2)}, u32[]{:S(2)}) async-start(bf16[64,16,1024]{2,1,0:T(8,128)(2,1)} %bitcast.74), calls=%async_computation.2 | async-start | bytes 4194304 | tf_op jit(solution)/shard_map/all_to_all | solution.py:130
  249.2 47.6 %reduce-scatter.5.cloned.1.call-start = ((), (), s32[]{:S(2)}) async-start(), calls=%async_computation.7 | async-start | bytes 1769472 | tf_op jit(solution)/shard_map/reduce_scatter | solution.py:135
  254.2 0.7 copy-start.3
Sparse Core Ops, SparseCore 0:
  203.4 39.9 reduce-scatter.6
  254.4 42.3 reduce-scatter.4
